TPU v7x, 512 devices: a whole 4x4x16 slice. The times are simulated.
512 devices in a mesh: ctx: 64 (over z, y), tp: 8 (over x, core).
Axes of the slice: x: 4, y: 4, z: 16, core: 2. Of those that a mesh axis runs over, the one named last changes fastest.
Arguments:
- features: bfloat16 [3, 4096, 8192], P(None, 'ctx', 'tp'), may hold values from -6 to 6
- short_weight: float32 [3, 3, 8192], P(None, None, 'tp'), may hold values from -3 to 3
- decay_rate: float32 [512, 16], P('tp'), may hold values from 0.00012207031 to 0.03
- residue: float32 [512, 16], P('tp'), may hold values from -3 to 3
- skip_gain: float32 [8192], P('tp'), may hold values from -1 to 1
- out_weight: bfloat16 [8192, 4096], P('tp', 'ctx'), may hold values from -0.1875 to 0.1875
Outputs:
- mixed_out: bfloat16 [4096, 4096], P('ctx', 'tp')
All inputs are finite; a program needn't handle non-finite values.
Results may differ from a plain program's by a relative error of at most 0.006.
Values may be sent and summed in bfloat16 or wider, within the bound.
No kernel may reach another device: no remote copies, remote signals or barrier semaphores. Data moves between devices by JAX's collectives and lax.ppermute only.
A program may use at most 128 MiB of HBM per device.

v0:
```python
import jax
import jax.numpy as jnp
import numpy as np
from jax import lax
from jax.sharding import Mesh
from jax.sharding import PartitionSpec as P

CTX = ("chi", "clo")


def shifted(value, axis, count, by):
    pairs = [(i, i + by) for i in range(count) if i + by < count]
    return lax.ppermute(value, axis, pairs)


def rotated(value, axis, count, by):
    return lax.ppermute(value, axis, [(i, (i + by) % count) for i in range(count)])


def digit_rotated(value, count, stride, size, by):
    pairs = []
    for i in range(count):
        d = i // stride % size
        pairs.append((i, i + ((d + by) % size - d) * stride))
    return lax.ppermute(value, CTX, pairs)


def scan_levels(count):
    levels = []
    while count > 1:
        size = 4 if count % 4 == 0 else count
        levels.append(size)
        count //= size
    return levels


def make_per_device(n_ctx, n_tp):
    n_lo = n_ctx // n_tp

    def per_device(features, short_weight, decay_rate, residue, skip_gain, out_weight):
        rows = features.shape[1]
        chans = features.shape[2]
        groups = decay_rate.shape[0]
        width = chans // groups
        taps = short_weight.shape[1]
        chi = lax.axis_index("chi")
        clo = lax.axis_index("clo")
        me = chi * n_lo + clo
        tp = lax.axis_index("tp")
        weight = lax.all_gather(out_weight, "chi", axis=1, tiled=True)
        weight = weight.reshape(chans, n_tp, -1)
        rim = shifted(features[:, rows - (taps - 1) :, :], CTX, n_ctx, 1)
        extended = jnp.concatenate([rim, features], axis=1)
        conv = jnp.zeros(features.shape, jnp.float32)
        for j in range(taps):
            conv = conv + short_weight[:, j][:, None, :] * extended[
                :, taps - 1 - j : taps - 1 - j + rows, :
            ].astype(jnp.float32)
        q_lane = conv[0]
        gated = (conv[1] * conv[2]).astype(jnp.bfloat16)
        gated_wide = gated.astype(jnp.float32)
        coef = residue * jnp.sqrt(-jnp.expm1(-2.0 * decay_rate))
        lags = jnp.arange(rows, dtype=jnp.float32)
        near_filter = jnp.sum(
            coef[:, :, None] * jnp.exp(-decay_rate[:, :, None] * lags[None, None, :]), axis=1
        ).astype(jnp.bfloat16)
        index = np.arange(rows)
        onehot = (index[None, :, None] - index[None, None, :] == index[:, None, None]).astype(
            np.float32
        )
        onehot = jnp.asarray(onehot.reshape(rows, rows * rows), jnp.bfloat16)
        toeplitz = jnp.dot(near_filter, onehot, preferred_element_type=jnp.float32)
        toeplitz = toeplitz.astype(jnp.bfloat16).reshape(groups, rows, rows)
        near = jnp.einsum(
            "gts,sgw->tgw",
            toeplitz,
            gated.reshape(rows, groups, width),
            preferred_element_type=jnp.float32,
        ).reshape(rows, chans)
        rate_c = jnp.repeat(decay_rate.T, width, axis=1)
        coef_c = jnp.repeat(coef.T, width, axis=1)

        def decay(blocks):
            return jnp.exp(-rate_c * (rows * blocks.astype(jnp.float32)))

        end_basis = jnp.exp(-rate_c[None] * (rows - 1.0 - lags)[:, None, None])
        own_state = jnp.sum(end_basis * gated_wide[:, None, :], axis=0)
        before = jnp.zeros_like(own_state)
        total = own_state
        stride = 1
        for size in scan_levels(n_ctx):
            d = me // stride % size
            r = me % stride
            merged = decay((size - 1 - d) * stride) * total
            for by in range(1, size):
                got = digit_rotated(total, n_ctx, stride, size, by)
                src = (d - by) % size
                before = before + jnp.where(
                    by <= d, decay((by - 1) * stride + r) * got, jnp.zeros_like(got)
                )
                merged = merged + decay((size - 1 - src) * stride) * got
            total = merged
            stride *= size
        far_basis = coef_c[None] * jnp.exp(-rate_c[None] * (lags + 1.0)[:, None, None])
        far = jnp.sum(far_basis * before[None], axis=1)
        mixed = (q_lane * (near + far + skip_gain[None, :] * gated_wide)).astype(jnp.bfloat16)
        spread = jnp.broadcast_to(mixed[None], (n_lo,) + mixed.shape)
        tokens = lax.all_to_all(spread, "clo", 0, 0, tiled=True)
        partial = jnp.einsum("ktc,cqo->qkto", tokens, weight, preferred_element_type=jnp.float32)
        pieces = lax.all_to_all(partial, "tp", 0, 0, tiled=True)
        summed = jnp.sum(pieces, axis=0).astype(jnp.bfloat16)
        back = lax.all_to_all(summed, "clo", 0, 0, tiled=True)
        return back.transpose(1, 0, 2).reshape(rows, -1)

    return per_device


def solution(mesh):
    n_ctx = mesh.shape["ctx"]
    n_tp = mesh.shape["tp"]
    devices = np.asarray(mesh.devices).reshape(n_tp, n_ctx // n_tp, n_tp)
    split = Mesh(devices, ("chi", "clo", "tp"))
    placed = (
        P(None, CTX, "tp"),
        P(None, None, "tp"),
        P("tp", None),
        P("tp", None),
        P("tp"),
        P("tp", CTX),
    )
    return jax.shard_map(
        make_per_device(n_ctx, n_tp),
        mesh=split,
        in_specs=placed,
        out_specs=P(CTX, "tp"),
        check_vma=False,
    )
```

profile of v0, /device:TPU:2, one launch (start us, length us, event | category | flops | bytes accessed | tf_op | source)
XLA Modules:
  0.0 183.9 jit_solution(3685164026990246933)
XLA Ops:
  6.5 0.8 slice.29
  7.4 3.5 %collective-permute-start = (bf16[3,2,1024]{2,1,0:T(2,128)(2,1)S(1)}, bf16[3,2,1024]{2,1,0:T(2,128)(2,1)S(1)}, u32[]{:S(2)}, u32[]{:S(2)}) collective-permute-start(bf16[3,2,1024]{2,1,0:T(2,128)(2,1)S(1)} %slice.29), channel_id=1, source_target_pairs={{0,8},{8,16},{16,24},{24,32},{32,40},{40,48},{48,56},{56,64},{64,7... | collective-permute-start | bytes 36872 | tf_op jit(solution)/shard_map/ppermute | solution.py:13
  10.8 0.9 fusion.9
  11.8 0.7 negate_bitcast_fusion
  12.5 0.1 copy.39
  12.6 0.1 copy.40
  12.7 0.4 multiply_reduce_fusion.2
  13.1 0.2 broadcast_in_dim.9
  13.3 0.3 neg.20
  13.6 0.0 copy-start
  13.6 0.0 collective-permute-done
  13.6 1.8 multiply_add_fusion
  15.5 0.7 multiply_reduce_fusion.1
  16.2 3.5 %collective-permute-start.1 = (f32[16,1024]{1,0:T(8,128)S(1)}, f32[16,1024]{1,0:T(8,128)S(1)}, u32[]{:S(2)}, u32[]{:S(2)}) collective-permute-start(f32[16,1024]{1,0:T(8,128)S(1)} %multiply_reduce_fusion.1), channel_id=1, source_target_pairs={{0,8},{8,16},{16,24},{24,0},{32,40},{40,48},{48,56},{56,32},{64,72... | collective-permute-start | bytes 196616 | tf_op jit(solution)/shard_map/ppermute | solution.py:25
  19.7 4.8 %collective-permute-start.2 = (f32[16,1024]{1,0:T(8,128)S(1)}, f32[16,1024]{1,0:T(8,128)S(1)}, u32[]{:S(2)}, u32[]{:S(2)}) collective-permute-start(f32[16,1024]{1,0:T(8,128)S(1)} %multiply_reduce_fusion.1), channel_id=1, source_target_pairs={{0,16},{8,24},{16,0},{24,8},{32,48},{40,56},{48,32},{56,40},{64,80... | collective-permute-start | bytes 196616 | tf_op jit(solution)/shard_map/ppermute | solution.py:25
  24.5 3.0 %collective-permute-start.3 = (f32[16,1024]{1,0:T(8,128)S(1)}, f32[16,1024]{1,0:T(8,128)S(1)}, u32[]{:S(2)}, u32[]{:S(2)}) collective-permute-start(f32[16,1024]{1,0:T(8,128)S(1)} %multiply_reduce_fusion.1), channel_id=1, source_target_pairs={{0,24},{8,0},{16,8},{24,16},{32,56},{40,32},{48,40},{56,48},{64,88... | collective-permute-start | bytes 196616 | tf_op jit(solution)/shard_map/ppermute | solution.py:25
  27.5 0.0 copy-done
  27.5 0.3 convolution_convert_fusion
  28.0 0.2 broadcast_in_dim.8
  28.2 0.3 mul.365
  28.5 1.1 reshape.75
  29.6 0.0 collective-permute-done.1
  29.6 0.0 collective-permute-done.2
  29.6 1.1 collective-permute-done.3
  30.7 3.8 %collective-permute-start.4 = (f32[16,1024]{1,0:T(8,128)S(1)}, f32[16,1024]{1,0:T(8,128)S(1)}, u32[]{:S(2)}, u32[]{:S(2)}) collective-permute-start(f32[16,1024]{1,0:T(8,128)S(1)} %multiply_add_fusion.2), channel_id=1, source_target_pairs={{0,32},{8,40},{16,48},{24,56},{32,64},{40,72},{48,80},{56,88},{64,... | collective-permute-start | bytes 196616 | tf_op jit(solution)/shard_map/ppermute | solution.py:25
  34.6 6.4 %collective-permute-start.5 = (f32[16,1024]{1,0:T(8,128)S(1)}, f32[16,1024]{1,0:T(8,128)S(1)}, u32[]{:S(2)}, u32[]{:S(2)}) collective-permute-start(f32[16,1024]{1,0:T(8,128)S(1)} %multiply_add_fusion.2), channel_id=1, source_target_pairs={{0,64},{8,72},{16,80},{24,88},{32,96},{40,104},{48,112},{56,120},{... | collective-permute-start | bytes 196616 | tf_op jit(solution)/shard_map/ppermute | solution.py:25
  41.0 1.9 %collective-permute-start.6 = (f32[16,1024]{1,0:T(8,128)S(1)}, f32[16,1024]{1,0:T(8,128)S(1)}, u32[]{:S(2)}, u32[]{:S(2)}) collective-permute-start(f32[16,1024]{1,0:T(8,128)S(1)} %multiply_add_fusion.2), channel_id=1, source_target_pairs={{0,96},{8,104},{16,112},{24,120},{32,0},{40,8},{48,16},{56,24},{64... | collective-permute-start | bytes 196616 | tf_op jit(solution)/shard_map/ppermute | solution.py:25
  42.9 0.2 copy.38
  43.1 0.0 collective-permute-done.4
  43.1 1.3 collective-permute-done.5
  44.4 2.7 %collective-permute-done.6 = f32[16,1024]{1,0:T(8,128)S(1)} collective-permute-done((f32[16,1024]{1,0:T(8,128)S(1)}, f32[16,1024]{1,0:T(8,128)S(1)}, u32[]{:S(2)}, u32[]{:S(2)}) %collective-permute-start.6) | collective-permute-done | bytes 65568 | tf_op jit(solution)/shard_map/ppermute | solution.py:25
  47.2 9.1 %collective-permute-start.7 = (f32[16,1024]{1,0:T(8,128)S(1)}, f32[16,1024]{1,0:T(8,128)S(1)}, u32[]{:S(2)}, u32[]{:S(2)}) collective-permute-start(f32[16,1024]{1,0:T(8,128)S(1)} %multiply_add_fusion.1), channel_id=1, source_target_pairs={{0,128},{8,136},{16,144},{24,152},{32,160},{40,168},{48,176},{56,1... | collective-permute-start | bytes 196616 | tf_op jit(solution)/shard_map/ppermute | solution.py:25
  56.3 7.2 %collective-permute-start.8 = (f32[16,1024]{1,0:T(8,128)S(1)}, f32[16,1024]{1,0:T(8,128)S(1)}, u32[]{:S(2)}, u32[]{:S(2)}) collective-permute-start(f32[16,1024]{1,0:T(8,128)S(1)} %multiply_add_fusion.1), channel_id=1, source_target_pairs={{0,256},{8,264},{16,272},{24,280},{32,288},{40,296},{48,304},{56,3... | collective-permute-start | bytes 196616 | tf_op jit(solution)/shard_map/ppermute | solution.py:25
  63.4 5.5 %collective-permute-start.9 = (f32[16,1024]{1,0:T(8,128)S(1)}, f32[16,1024]{1,0:T(8,128)S(1)}, u32[]{:S(2)}, u32[]{:S(2)}) collective-permute-start(f32[16,1024]{1,0:T(8,128)S(1)} %multiply_add_fusion.1), channel_id=1, source_target_pairs={{0,384},{8,392},{16,400},{24,408},{32,416},{40,424},{48,432},{56,4... | collective-permute-start | bytes 196616 | tf_op jit(solution)/shard_map/ppermute | solution.py:25
  68.9 0.6 fusion.10
  69.5 0.0 copy-start.1
  69.5 0.2 copy.41
  69.8 0.0 collective-permute-done.7
  69.8 1.8 collective-permute-done.8
  71.5 4.0 %collective-permute-done.9 = f32[16,1024]{1,0:T(8,128)S(1)} collective-permute-done((f32[16,1024]{1,0:T(8,128)S(1)}, f32[16,1024]{1,0:T(8,128)S(1)}, u32[]{:S(2)}, u32[]{:S(2)}) %collective-permute-start.9) | collective-permute-done | bytes 65568 | tf_op jit(solution)/shard_map/ppermute | solution.py:25
  75.5 0.1 select_add_fusion
  75.7 1.4 multiply_reduce_fusion
  77.1 0.0 copy-done.1
  77.1 0.1 fusion.6
  77.2 1.2 broadcast_in_dim.11
  78.3 3.7 %all-to-all-start = ((bf16[8,64,1024]{2,1,0:T(8,128)(2,1)}), bf16[8,64,1024]{2,1,0:T(8,128)(2,1)S(1)}, u32[]{:S(2)}, u32[]{:S(2)}) async-start(bf16[8,64,1024]{2,1,0:T(8,128)(2,1)} %broadcast_in_dim.11), calls=%async_computation | async-start | bytes 2097152 | tf_op jit(solution)/shard_map/all_to_all | solution.py:108
  82.1 0.0 all-gather.2.cloned.1.call-start
  82.1 0.7 all-gather.2.cloned.1.call-update
  82.8 52.5 %all-gather.2.cloned.1.call-done = bf16[1024,512]{0,1:T(8,128)(2,1)} async-done(((bf16[1024,64]{0,1:T(8,128)(2,1)}), bf16[1024,512]{0,1:T(8,128)(2,1)}) %all-gather.2.cloned.1.call-update) | async-done | bytes 1048592 | tf_op jit(solution)/shard_map/all_gather | solution.py:50
  135.3 0.0 all-to-all-done
  135.3 2.5 %convolution_bitcast_fusion = f32[8,8,64,64]{3,2,0,1:T(8,128)S(1)} fusion(bf16[1024,8,64,1]{0,2,1,3:T(8,128)(2,1)} %bitcast.45, bf16[8,64,1024]{2,1,0:T(8,128)(2,1)S(1)} %all-to-all-done), kind=kOutput, calls=%fused_computation.3 | convolution fusion | flops 536870912 | bytes 3145728 | tf_op jit(solution)/shard_map/ktc,cqo->qkto/dot_general | solution.py:109
  137.8 0.2 copy.42
  138.1 1.3 reshape.82
  139.4 19.1 %all_to_all.15 = f32[8,1,32768]{2,1,0:T(1,128)S(1)} all-to-all(f32[8,1,32768]{2,1,0:T(1,128)S(1)} %reshape.82), channel_id=1, replica_groups=mesh['chi'=8,'clo'=8,'tp'=8] {'tp'}, dimensions={0} | all-to-all | bytes 2097152 | tf_op jit(solution)/shard_map/all_to_all | solution.py:110
  158.5 0.5 broadcast.33
  159.1 3.1 %reduce = f32[8,32768]{1,0:T(8,128)S(1)} reduce(f32[8,1,32768]{2,1,0:T(1,128)S(1)} %all_to_all.15, f32[]{:T(128)} %broadcast.33), dimensions={1}, to_apply=%all_to_all.10.reduce_sub_computation | reduce | bytes 2097156 | tf_op jit(solution)/shard_map/all_to_all | solution.py:110
  162.2 0.8 reshape.83
  163.0 0.2 reduce_sum.42
  163.3 0.2 reshape.84
  163.4 12.6 %all_to_all.16 = bf16[8,2,2048]{2,1,0:T(2,128)(2,1)S(1)} all-to-all(bf16[8,2,2048]{2,1,0:T(2,128)(2,1)S(1)} %reshape.84), channel_id=1, replica_groups=mesh['chi'=8,'clo'=8,'tp'=8] {'clo'}, dimensions={0} | all-to-all | bytes 131072 | tf_op jit(solution)/shard_map/all_to_all | solution.py:112
  176.0 0.1 reshape.85
  176.2 0.1 copy.44
  176.3 0.8 reshape.78
  (7 shorter events, 0.2 us)
Async XLA Ops:
  7.4 6.2 %collective-permute-start = (bf16[3,2,1024]{2,1,0:T(2,128)(2,1)S(1)}, bf16[3,2,1024]{2,1,0:T(2,128)(2,1)S(1)}, u32[]{:S(2)}, u32[]{:S(2)}) collective-permute-start(bf16[3,2,1024]{2,1,0:T(2,128)(2,1)S(1)} %slice.29), channel_id=1, source_target_pairs={{0,8},{8,16},{16,24},{24,32},{32,40},{40,48},{48,56},{56,64},{64,7... | collective-permute-start | bytes 36872 | tf_op jit(solution)/shard_map/ppermute | solution.py:13
  13.6 13.9 %copy-start = (bf16[64,4096]{1,0:T(8,128)(2,1)S(1)}, bf16[64,4096]{1,0:T(8,128)(2,1)}, u32[]{:S(2)}) copy-start(bf16[64,4096]{1,0:T(8,128)(2,1)} %constant.139.clone) | copy-start | bytes 1572868
  16.2 13.4 %collective-permute-start.1 = (f32[16,1024]{1,0:T(8,128)S(1)}, f32[16,1024]{1,0:T(8,128)S(1)}, u32[]{:S(2)}, u32[]{:S(2)}) collective-permute-start(f32[16,1024]{1,0:T(8,128)S(1)} %multiply_reduce_fusion.1), channel_id=1, source_target_pairs={{0,8},{8,16},{16,24},{24,0},{32,40},{40,48},{48,56},{56,32},{64,72... | collective-permute-start | bytes 196616 | tf_op jit(solution)/shard_map/ppermute | solution.py:25
  19.7 9.9 %collective-permute-start.2 = (f32[16,1024]{1,0:T(8,128)S(1)}, f32[16,1024]{1,0:T(8,128)S(1)}, u32[]{:S(2)}, u32[]{:S(2)}) collective-permute-start(f32[16,1024]{1,0:T(8,128)S(1)} %multiply_reduce_fusion.1), channel_id=1, source_target_pairs={{0,16},{8,24},{16,0},{24,8},{32,48},{40,56},{48,32},{56,40},{64,80... | collective-permute-start | bytes 196616 | tf_op jit(solution)/shard_map/ppermute | solution.py:25
  24.5 6.2 %collective-permute-start.3 = (f32[16,1024]{1,0:T(8,128)S(1)}, f32[16,1024]{1,0:T(8,128)S(1)}, u32[]{:S(2)}, u32[]{:S(2)}) collective-permute-start(f32[16,1024]{1,0:T(8,128)S(1)} %multiply_reduce_fusion.1), channel_id=1, source_target_pairs={{0,24},{8,0},{16,8},{24,16},{32,56},{40,32},{48,40},{56,48},{64,88... | collective-permute-start | bytes 196616 | tf_op jit(solution)/shard_map/ppermute | solution.py:25
  30.7 12.3 %collective-permute-start.4 = (f32[16,1024]{1,0:T(8,128)S(1)}, f32[16,1024]{1,0:T(8,128)S(1)}, u32[]{:S(2)}, u32[]{:S(2)}) collective-permute-start(f32[16,1024]{1,0:T(8,128)S(1)} %multiply_add_fusion.2), channel_id=1, source_target_pairs={{0,32},{8,40},{16,48},{24,56},{32,64},{40,72},{48,80},{56,88},{64,... | collective-permute-start | bytes 196616 | tf_op jit(solution)/shard_map/ppermute | solution.py:25
  34.6 9.8 %collective-permute-start.5 = (f32[16,1024]{1,0:T(8,128)S(1)}, f32[16,1024]{1,0:T(8,128)S(1)}, u32[]{:S(2)}, u32[]{:S(2)}) collective-permute-start(f32[16,1024]{1,0:T(8,128)S(1)} %multiply_add_fusion.2), channel_id=1, source_target_pairs={{0,64},{8,72},{16,80},{24,88},{32,96},{40,104},{48,112},{56,120},{... | collective-permute-start | bytes 196616 | tf_op jit(solution)/shard_map/ppermute | solution.py:25
  41.0 6.2 %collective-permute-start.6 = (f32[16,1024]{1,0:T(8,128)S(1)}, f32[16,1024]{1,0:T(8,128)S(1)}, u32[]{:S(2)}, u32[]{:S(2)}) collective-permute-start(f32[16,1024]{1,0:T(8,128)S(1)} %multiply_add_fusion.2), channel_id=1, source_target_pairs={{0,96},{8,104},{16,112},{24,120},{32,0},{40,8},{48,16},{56,24},{64... | collective-permute-start | bytes 196616 | tf_op jit(solution)/shard_map/ppermute | solution.py:25
  47.2 22.6 %collective-permute-start.7 = (f32[16,1024]{1,0:T(8,128)S(1)}, f32[16,1024]{1,0:T(8,128)S(1)}, u32[]{:S(2)}, u32[]{:S(2)}) collective-permute-start(f32[16,1024]{1,0:T(8,128)S(1)} %multiply_add_fusion.1), channel_id=1, source_target_pairs={{0,128},{8,136},{16,144},{24,152},{32,160},{40,168},{48,176},{56,1... | collective-permute-start | bytes 196616 | tf_op jit(solution)/shard_map/ppermute | solution.py:25
  56.3 15.2 %collective-permute-start.8 = (f32[16,1024]{1,0:T(8,128)S(1)}, f32[16,1024]{1,0:T(8,128)S(1)}, u32[]{:S(2)}, u32[]{:S(2)}) collective-permute-start(f32[16,1024]{1,0:T(8,128)S(1)} %multiply_add_fusion.1), channel_id=1, source_target_pairs={{0,256},{8,264},{16,272},{24,280},{32,288},{40,296},{48,304},{56,3... | collective-permute-start | bytes 196616 | tf_op jit(solution)/shard_map/ppermute | solution.py:25
  63.4 12.1 %collective-permute-start.9 = (f32[16,1024]{1,0:T(8,128)S(1)}, f32[16,1024]{1,0:T(8,128)S(1)}, u32[]{:S(2)}, u32[]{:S(2)}) collective-permute-start(f32[16,1024]{1,0:T(8,128)S(1)} %multiply_add_fusion.1), channel_id=1, source_target_pairs={{0,384},{8,392},{16,400},{24,408},{32,416},{40,424},{48,432},{56,4... | collective-permute-start | bytes 196616 | tf_op jit(solution)/shard_map/ppermute | solution.py:25
  69.5 7.5 %copy-start.1 = (f32[1024]{0:T(1024)S(1)}, f32[1024]{0:T(1024)}, u32[]{:S(2)}) copy-start(f32[1024]{0:T(1024)} %param.11) | copy-start | bytes 12292
  78.3 57.0 %all-to-all-start = ((bf16[8,64,1024]{2,1,0:T(8,128)(2,1)}), bf16[8,64,1024]{2,1,0:T(8,128)(2,1)S(1)}, u32[]{:S(2)}, u32[]{:S(2)}) async-start(bf16[8,64,1024]{2,1,0:T(8,128)(2,1)} %broadcast_in_dim.11), calls=%async_computation | async-start | bytes 2097152 | tf_op jit(solution)/shard_map/all_to_all | solution.py:108
  82.1 53.2 %all-gather.2.cloned.1.call-start = ((), (), s32[]{:S(2)}) async-start(), calls=%async_computation.3 | async-start | bytes 1179648 | tf_op jit(solution)/shard_map/all_gather | solution.py:50
Sparse Core Ops, SparseCore 0:
  85.0 50.3 all-gather.1
where the time goes:
time: 185 us; the launch traced here: 184 us
  waiting for transfers between devices  64.1 us (35%)
  starting transfers between devices  52.4 us (28%)
  blocking collectives  31.7 us (17%)
  between operations  13.9 us (8%)
  local copies, waits for them, and re-layouts  9.62 us (5%)
  other arithmetic  8.77 us (5%)
  matrix products  3.41 us (2%)
    all_gather x1, waiting for transfers between devices, per_device(): weight = lax.all_gather(out_weight, 'chi', axis=1, tiled=True)  52.5 us
    ppermute x9, starting transfers between devices, digit_rotated(): return lax.ppermute(value, CTX, pairs)  45.1 us
    all_to_all x1, blocking collectives, per_device(): pieces = lax.all_to_all(partial, 'tp', 0, 0, tiled=True)  19.1 us
    all_to_all x1, blocking collectives, per_device(): back = lax.all_to_all(summed, 'clo', 0, 0, tiled=True)  12.6 us
    ppermute x9, waiting for transfers between devices, digit_rotated(): return lax.ppermute(value, CTX, pairs)  10.9 us
    all_to_all x1, starting transfers between devices, per_device(): tokens = lax.all_to_all(spread, 'clo', 0, 0, tiled=True)  3.75 us
  transfers between devices with their start and end apart: 12, of which 6 were waited for; matrix products, arithmetic and copies ran while one was open for 3% of the time, Pallas kernels for 0%

commit v1 on v0

--- a/solution.py
+++ b/solution.py
@@ -1,3 +1,4 @@
+import functools
 import jax
 import jax.numpy as jnp
 import numpy as np
@@ -6,6 +7,21 @@
 from jax.sharding import PartitionSpec as P
 
 CTX = ("chi", "clo")
+
+
+def clear_entries(my_tile, chip_axis):
+    return jnp.concatenate(
+        jax.lax.all_to_all(
+            jnp.stack([my_tile for _ in range(jax.lax.psum(1, axis_name=chip_axis))], axis=0),
+            axis_name=chip_axis,
+            split_axis=0,
+            concat_axis=0,
+        ),
+        axis=1,
+    )
+
+
+heads_rest = functools.partial(clear_entries, chip_axis="chi")
 
 
 def shifted(value, axis, count, by):
@@ -47,7 +63,7 @@
         clo = lax.axis_index("clo")
         me = chi * n_lo + clo
         tp = lax.axis_index("tp")
-        weight = lax.all_gather(out_weight, "chi", axis=1, tiled=True)
+        weight = heads_rest(out_weight)
         weight = weight.reshape(chans, n_tp, -1)
         rim = shifted(features[:, rows - (taps - 1) :, :], CTX, n_ctx, 1)
         extended = jnp.concatenate([rim, features], axis=1)

time: 185 us -> 178 us (0.962)
  the two profiles are of different devices: /device:TPU:2 before, /device:TPU:64 now
where the time goes in v1:
time: 178 us; the launch traced here: 177 us
  starting transfers between devices  59.3 us (33%)
  waiting for transfers between devices  50.7 us (28%)
  blocking collectives  47.7 us (27%)
  local copies, waits for them, and re-layouts  8.98 us (5%)
  other arithmetic  6.51 us (4%)
  matrix products  3.4 us (2%)
    ppermute x1, waiting for transfers between devices, shifted(): return lax.ppermute(value, axis, pairs)  42.4 us
    ppermute x9, starting transfers between devices, digit_rotated(): return lax.ppermute(value, CTX, pairs)  41.1 us
    all_to_all x1, blocking collectives, per_device(): pieces = lax.all_to_all(partial, 'tp', 0, 0, tiled=True)  20.1 us
    all_to_all x1, blocking collectives, per_device(): tokens = lax.all_to_all(spread, 'clo', 0, 0, tiled=True)  18.7 us
    all_to_all x1, starting transfers between devices, clear_entries(): jax.lax.all_to_all(jnp.stack([my_tile for _ in range(jax.lax.psum(1, axis...  14.7 us
    all_to_all x1, blocking collectives, per_device(): back = lax.all_to_all(summed, 'clo', 0, 0, tiled=True)  8.89 us
    ppermute x9, waiting for transfers between devices, digit_rotated(): return lax.ppermute(value, CTX, pairs)  8.26 us
  transfers between devices with their start and end apart: 11, of which 6 were waited for; matrix products, arithmetic and copies ran while one was open for 4% of the time, Pallas kernels for 0%

profile of v1, /device:TPU:64, one launch (start us, length us, event | category | flops | bytes accessed | tf_op | source)
XLA Modules:
  0.0 177.2 jit_solution(11113809846797515461)
XLA Ops:
  0.0 0.0 copy-start.1
  0.0 0.0 copy-start.2
  0.0 2.1 %stack.2 = bf16[8,1024,64]{1,2,0:T(8,128)(2,1)} broadcast(bf16[1024,64]{0,1:T(8,128)(2,1)} %param.12), dimensions={1,2} | broadcast | bytes 1179648 | tf_op jit(solution)/shard_map/stack | solution.py:15
  2.1 14.7 %all-to-all-start.1 = ((bf16[8,1024,64]{1,2,0:T(8,128)(2,1)}), bf16[8,1024,64]{1,2,0:T(8,128)(2,1)}, u32[]{:S(2)}, u32[]{:S(2)}) async-start(bf16[8,1024,64]{1,2,0:T(8,128)(2,1)} %stack.2), calls=%async_computation.1 | async-start | bytes 2097152 | tf_op jit(solution)/shard_map/all_to_all | solution.py:14
  16.9 0.0 copy-done.1
  16.9 3.5 %collective-permute-start = (bf16[3,2,1024]{2,1,0:T(2,128)(2,1)S(1)}, bf16[3,2,1024]{2,1,0:T(2,128)(2,1)S(1)}, u32[]{:S(2)}, u32[]{:S(2)}) collective-permute-start(bf16[3,2,1024]{2,1,0:T(2,128)(2,1)S(1)} %slice.29), channel_id=1, source_target_pairs={{0,8},{8,16},{16,24},{24,32},{32,40},{40,48},{48,56},{56,64},{64,7... | collective-permute-start | bytes 36872 | tf_op jit(solution)/shard_map/ppermute | solution.py:29
  20.4 0.0 copy-done.4
  20.4 0.0 copy-done.3
  20.4 0.1 copy.39
  20.5 0.1 copy.40
  20.6 0.4 multiply_reduce_fusion.2
  21.0 0.0 copy-done.2
  21.1 0.2 broadcast_in_dim.9
  21.3 0.3 neg.20
  21.5 0.0 copy-start
  21.5 42.4 %collective-permute-done = bf16[3,2,1024]{2,1,0:T(2,128)(2,1)S(1)} collective-permute-done((bf16[3,2,1024]{2,1,0:T(2,128)(2,1)S(1)}, bf16[3,2,1024]{2,1,0:T(2,128)(2,1)S(1)}, u32[]{:S(2)}, u32[]{:S(2)}) %collective-permute-start) | collective-permute-done | bytes 12320 | tf_op jit(solution)/shard_map/ppermute | solution.py:29
  64.0 0.3 multiply_add_fusion
  64.3 0.7 multiply_reduce_fusion.1
  65.1 1.9 %collective-permute-start.1 = (f32[16,1024]{1,0:T(8,128)S(1)}, f32[16,1024]{1,0:T(8,128)S(1)}, u32[]{:S(2)}, u32[]{:S(2)}) collective-permute-start(f32[16,1024]{1,0:T(8,128)S(1)} %multiply_reduce_fusion.1), channel_id=1, source_target_pairs={{0,8},{8,16},{16,24},{24,0},{32,40},{40,48},{48,56},{56,32},{64,72... | collective-permute-start | bytes 196616 | tf_op jit(solution)/shard_map/ppermute | solution.py:41
  67.0 1.9 %collective-permute-start.2 = (f32[16,1024]{1,0:T(8,128)S(1)}, f32[16,1024]{1,0:T(8,128)S(1)}, u32[]{:S(2)}, u32[]{:S(2)}) collective-permute-start(f32[16,1024]{1,0:T(8,128)S(1)} %multiply_reduce_fusion.1), channel_id=1, source_target_pairs={{0,16},{8,24},{16,0},{24,8},{32,48},{40,56},{48,32},{56,40},{64,80... | collective-permute-start | bytes 196616 | tf_op jit(solution)/shard_map/ppermute | solution.py:41
  68.9 5.1 %collective-permute-start.3 = (f32[16,1024]{1,0:T(8,128)S(1)}, f32[16,1024]{1,0:T(8,128)S(1)}, u32[]{:S(2)}, u32[]{:S(2)}) collective-permute-start(f32[16,1024]{1,0:T(8,128)S(1)} %multiply_reduce_fusion.1), channel_id=1, source_target_pairs={{0,24},{8,0},{16,8},{24,16},{32,56},{40,32},{48,40},{56,48},{64,88... | collective-permute-start | bytes 196616 | tf_op jit(solution)/shard_map/ppermute | solution.py:41
  74.1 0.0 copy-done
  74.1 0.3 convolution_convert_fusion
  74.6 0.2 broadcast_in_dim.8
  74.8 0.3 mul.365
  75.0 1.1 reshape.77
  76.2 0.0 collective-permute-done.1
  76.2 0.0 collective-permute-done.2
  76.2 0.9 collective-permute-done.3
  77.2 3.5 %collective-permute-start.4 = (f32[16,1024]{1,0:T(8,128)S(1)}, f32[16,1024]{1,0:T(8,128)S(1)}, u32[]{:S(2)}, u32[]{:S(2)}) collective-permute-start(f32[16,1024]{1,0:T(8,128)S(1)} %multiply_add_fusion.2), channel_id=1, source_target_pairs={{0,32},{8,40},{16,48},{24,56},{32,64},{40,72},{48,80},{56,88},{64,... | collective-permute-start | bytes 196616 | tf_op jit(solution)/shard_map/ppermute | solution.py:41
  80.7 1.9 %collective-permute-start.5 = (f32[16,1024]{1,0:T(8,128)S(1)}, f32[16,1024]{1,0:T(8,128)S(1)}, u32[]{:S(2)}, u32[]{:S(2)}) collective-permute-start(f32[16,1024]{1,0:T(8,128)S(1)} %multiply_add_fusion.2), channel_id=1, source_target_pairs={{0,64},{8,72},{16,80},{24,88},{32,96},{40,104},{48,112},{56,120},{... | collective-permute-start | bytes 196616 | tf_op jit(solution)/shard_map/ppermute | solution.py:41
  82.6 3.4 %collective-permute-start.6 = (f32[16,1024]{1,0:T(8,128)S(1)}, f32[16,1024]{1,0:T(8,128)S(1)}, u32[]{:S(2)}, u32[]{:S(2)}) collective-permute-start(f32[16,1024]{1,0:T(8,128)S(1)} %multiply_add_fusion.2), channel_id=1, source_target_pairs={{0,96},{8,104},{16,112},{24,120},{32,0},{40,8},{48,16},{56,24},{64... | collective-permute-start | bytes 196616 | tf_op jit(solution)/shard_map/ppermute | solution.py:41
  86.0 0.2 copy.38
  86.2 0.0 collective-permute-done.4
  86.2 2.1 %collective-permute-done.5 = f32[16,1024]{1,0:T(8,128)S(1)} collective-permute-done((f32[16,1024]{1,0:T(8,128)S(1)}, f32[16,1024]{1,0:T(8,128)S(1)}, u32[]{:S(2)}, u32[]{:S(2)}) %collective-permute-start.5) | collective-permute-done | bytes 65568 | tf_op jit(solution)/shard_map/ppermute | solution.py:41
  88.3 0.5 collective-permute-done.6
  88.8 8.5 %collective-permute-start.7 = (f32[16,1024]{1,0:T(8,128)S(1)}, f32[16,1024]{1,0:T(8,128)S(1)}, u32[]{:S(2)}, u32[]{:S(2)}) collective-permute-start(f32[16,1024]{1,0:T(8,128)S(1)} %multiply_add_fusion.1), channel_id=1, source_target_pairs={{0,128},{8,136},{16,144},{24,152},{32,160},{40,168},{48,176},{56,1... | collective-permute-start | bytes 196616 | tf_op jit(solution)/shard_map/ppermute | solution.py:41
  97.3 9.3 %collective-permute-start.8 = (f32[16,1024]{1,0:T(8,128)S(1)}, f32[16,1024]{1,0:T(8,128)S(1)}, u32[]{:S(2)}, u32[]{:S(2)}) collective-permute-start(f32[16,1024]{1,0:T(8,128)S(1)} %multiply_add_fusion.1), channel_id=1, source_target_pairs={{0,256},{8,264},{16,272},{24,280},{32,288},{40,296},{48,304},{56,3... | collective-permute-start | bytes 196616 | tf_op jit(solution)/shard_map/ppermute | solution.py:41
  106.6 5.5 %collective-permute-start.9 = (f32[16,1024]{1,0:T(8,128)S(1)}, f32[16,1024]{1,0:T(8,128)S(1)}, u32[]{:S(2)}, u32[]{:S(2)}) collective-permute-start(f32[16,1024]{1,0:T(8,128)S(1)} %multiply_add_fusion.1), channel_id=1, source_target_pairs={{0,384},{8,392},{16,400},{24,408},{32,416},{40,424},{48,432},{56,4... | collective-permute-start | bytes 196616 | tf_op jit(solution)/shard_map/ppermute | solution.py:41
  112.1 0.6 fusion.11
  112.8 0.2 copy.41
  113.0 0.0 collective-permute-done.7
  113.0 1.5 collective-permute-done.8
  114.5 3.2 %collective-permute-done.9 = f32[16,1024]{1,0:T(8,128)S(1)} collective-permute-done((f32[16,1024]{1,0:T(8,128)S(1)}, f32[16,1024]{1,0:T(8,128)S(1)}, u32[]{:S(2)}, u32[]{:S(2)}) %collective-permute-start.9) | collective-permute-done | bytes 65568 | tf_op jit(solution)/shard_map/ppermute | solution.py:41
  117.7 0.1 select_add_fusion
  117.8 1.4 multiply_reduce_fusion
  119.3 0.0 copy-done.5
  119.3 0.1 fusion.7
  119.3 0.0 all-to-all-done.1
  119.4 0.1 broadcast_in_dim.11
  119.5 18.7 %all_to_all.20 = bf16[8,64,1024]{2,1,0:T(8,128)(2,1)S(1)} all-to-all(bf16[8,64,1024]{2,1,0:T(8,128)(2,1)S(1)} %broadcast_in_dim.11), channel_id=1, replica_groups=mesh['chi'=8,'clo'=8,'tp'=8] {'clo'}, dimensions={0} | all-to-all | bytes 2097152 | tf_op jit(solution)/shard_map/all_to_all | solution.py:124
  138.2 2.5 %convolution_bitcast_fusion = f32[8,8,64,64]{3,2,0,1:T(8,128)S(1)} fusion(bf16[8,1024,64]{1,2,0:T(8,128)(2,1)} %all-to-all-done.1, bf16[8,64,1024]{2,1,0:T(8,128)(2,1)S(1)} %all_to_all.20), kind=kOutput, calls=%fused_computation.3 | convolution fusion | flops 536870912 | bytes 3145728 | tf_op jit(solution)/shard_map/ktc,cqo->qkto/dot_general | solution.py:125
  140.7 0.2 copy.42
  141.0 1.3 reshape.84
  142.3 20.1 %all_to_all.21 = f32[8,1,32768]{2,1,0:T(1,128)S(1)} all-to-all(f32[8,1,32768]{2,1,0:T(1,128)S(1)} %reshape.84), channel_id=1, replica_groups=mesh['chi'=8,'clo'=8,'tp'=8] {'tp'}, dimensions={0} | all-to-all | bytes 2097152 | tf_op jit(solution)/shard_map/all_to_all | solution.py:126
  162.4 0.5 broadcast.35
  162.9 3.1 %reduce = f32[8,32768]{1,0:T(8,128)S(1)} reduce(f32[8,1,32768]{2,1,0:T(1,128)S(1)} %all_to_all.21, f32[]{:T(128)} %broadcast.35), dimensions={1}, to_apply=%all_to_all.14.reduce_sub_computation | reduce | bytes 2097156 | tf_op jit(solution)/shard_map/all_to_all | solution.py:126
  166.0 0.8 reshape.85
  166.9 0.2 reduce_sum.42
  167.1 0.2 reshape.86
  167.3 8.9 %all_to_all.22 = bf16[8,2,2048]{2,1,0:T(2,128)(2,1)S(1)} all-to-all(bf16[8,2,2048]{2,1,0:T(2,128)(2,1)S(1)} %reshape.86), channel_id=1, replica_groups=mesh['chi'=8,'clo'=8,'tp'=8] {'clo'}, dimensions={0} | all-to-all | bytes 131072 | tf_op jit(solution)/shard_map/all_to_all | solution.py:128
  176.1 0.1 reshape.87
  176.3 0.1 copy.44
  176.4 0.8 reshape.80
  (13 shorter events, 0.2 us)
Async XLA Ops:
  0.0 16.9 %copy-start.1 = (bf16[3,64,1024]{2,1,0:T(8,128)(2,1)S(1)}, bf16[3,64,1024]{2,1,0:T(8,128)(2,1)}, u32[]{:S(2)}) copy-start(bf16[3,64,1024]{2,1,0:T(8,128)(2,1)} %param.7) | copy-start | bytes 1179652
  0.0 20.4 %copy-start.4 = (f32[64,16]{0,1:T(8,128)S(1)}, f32[64,16]{0,1:T(8,128)}, u32[]{:S(2)}) copy-start(f32[64,16]{0,1:T(8,128)} %param.10) | copy-start | bytes 12292
  0.0 20.4 %copy-start.3 = (f32[64,16]{0,1:T(8,128)S(1)}, f32[64,16]{0,1:T(8,128)}, u32[]{:S(2)}) copy-start(f32[64,16]{0,1:T(8,128)} %param.9) | copy-start | bytes 12292
  0.0 21.0 %copy-start.2 = (f32[3,3,1024]{2,1,0:T(4,128)S(1)}, f32[3,3,1024]{2,1,0:T(4,128)}, u32[]{:S(2)}) copy-start(f32[3,3,1024]{2,1,0:T(4,128)} %param.8) | copy-start | bytes 110596
  2.1 117.2 %all-to-all-start.1 = ((bf16[8,1024,64]{1,2,0:T(8,128)(2,1)}), bf16[8,1024,64]{1,2,0:T(8,128)(2,1)}, u32[]{:S(2)}, u32[]{:S(2)}) async-start(bf16[8,1024,64]{1,2,0:T(8,128)(2,1)} %stack.2), calls=%async_computation.1 | async-start | bytes 2097152 | tf_op jit(solution)/shard_map/all_to_all | solution.py:14
  16.9 47.1 %collective-permute-start = (bf16[3,2,1024]{2,1,0:T(2,128)(2,1)S(1)}, bf16[3,2,1024]{2,1,0:T(2,128)(2,1)S(1)}, u32[]{:S(2)}, u32[]{:S(2)}) collective-permute-start(bf16[3,2,1024]{2,1,0:T(2,128)(2,1)S(1)} %slice.29), channel_id=1, source_target_pairs={{0,8},{8,16},{16,24},{24,32},{32,40},{40,48},{48,56},{56,64},{64,7... | collective-permute-start | bytes 36872 | tf_op jit(solution)/shard_map/ppermute | solution.py:29
  21.5 52.5 %copy-start = (bf16[64,4096]{1,0:T(8,128)(2,1)S(1)}, bf16[64,4096]{1,0:T(8,128)(2,1)}, u32[]{:S(2)}) copy-start(bf16[64,4096]{1,0:T(8,128)(2,1)} %constant.139.clone) | copy-start | bytes 1572868
  65.1 11.1 %collective-permute-start.1 = (f32[16,1024]{1,0:T(8,128)S(1)}, f32[16,1024]{1,0:T(8,128)S(1)}, u32[]{:S(2)}, u32[]{:S(2)}) collective-permute-start(f32[16,1024]{1,0:T(8,128)S(1)} %multiply_reduce_fusion.1), channel_id=1, source_target_pairs={{0,8},{8,16},{16,24},{24,0},{32,40},{40,48},{48,56},{56,32},{64,72... | collective-permute-start | bytes 196616 | tf_op jit(solution)/shard_map/ppermute | solution.py:41
  67.0 9.2 %collective-permute-start.2 = (f32[16,1024]{1,0:T(8,128)S(1)}, f32[16,1024]{1,0:T(8,128)S(1)}, u32[]{:S(2)}, u32[]{:S(2)}) collective-permute-start(f32[16,1024]{1,0:T(8,128)S(1)} %multiply_reduce_fusion.1), channel_id=1, source_target_pairs={{0,16},{8,24},{16,0},{24,8},{32,48},{40,56},{48,32},{56,40},{64,80... | collective-permute-start | bytes 196616 | tf_op jit(solution)/shard_map/ppermute | solution.py:41
  68.9 8.2 %collective-permute-start.3 = (f32[16,1024]{1,0:T(8,128)S(1)}, f32[16,1024]{1,0:T(8,128)S(1)}, u32[]{:S(2)}, u32[]{:S(2)}) collective-permute-start(f32[16,1024]{1,0:T(8,128)S(1)} %multiply_reduce_fusion.1), channel_id=1, source_target_pairs={{0,24},{8,0},{16,8},{24,16},{32,56},{40,32},{48,40},{56,48},{64,88... | collective-permute-start | bytes 196616 | tf_op jit(solution)/shard_map/ppermute | solution.py:41
  77.2 9.0 %collective-permute-start.4 = (f32[16,1024]{1,0:T(8,128)S(1)}, f32[16,1024]{1,0:T(8,128)S(1)}, u32[]{:S(2)}, u32[]{:S(2)}) collective-permute-start(f32[16,1024]{1,0:T(8,128)S(1)} %multiply_add_fusion.2), channel_id=1, source_target_pairs={{0,32},{8,40},{16,48},{24,56},{32,64},{40,72},{48,80},{56,88},{64,... | collective-permute-start | bytes 196616 | tf_op jit(solution)/shard_map/ppermute | solution.py:41
  80.7 7.6 %collective-permute-start.5 = (f32[16,1024]{1,0:T(8,128)S(1)}, f32[16,1024]{1,0:T(8,128)S(1)}, u32[]{:S(2)}, u32[]{:S(2)}) collective-permute-start(f32[16,1024]{1,0:T(8,128)S(1)} %multiply_add_fusion.2), channel_id=1, source_target_pairs={{0,64},{8,72},{16,80},{24,88},{32,96},{40,104},{48,112},{56,120},{... | collective-permute-start | bytes 196616 | tf_op jit(solution)/shard_map/ppermute | solution.py:41
  82.6 6.2 %collective-permute-start.6 = (f32[16,1024]{1,0:T(8,128)S(1)}, f32[16,1024]{1,0:T(8,128)S(1)}, u32[]{:S(2)}, u32[]{:S(2)}) collective-permute-start(f32[16,1024]{1,0:T(8,128)S(1)} %multiply_add_fusion.2), channel_id=1, source_target_pairs={{0,96},{8,104},{16,112},{24,120},{32,0},{40,8},{48,16},{56,24},{64... | collective-permute-start | bytes 196616 | tf_op jit(solution)/shard_map/ppermute | solution.py:41
  88.8 24.2 %collective-permute-start.7 = (f32[16,1024]{1,0:T(8,128)S(1)}, f32[16,1024]{1,0:T(8,128)S(1)}, u32[]{:S(2)}, u32[]{:S(2)}) collective-permute-start(f32[16,1024]{1,0:T(8,128)S(1)} %multiply_add_fusion.1), channel_id=1, source_target_pairs={{0,128},{8,136},{16,144},{24,152},{32,160},{40,168},{48,176},{56,1... | collective-permute-start | bytes 196616 | tf_op jit(solution)/shard_map/ppermute | solution.py:41
  97.3 17.2 %collective-permute-start.8 = (f32[16,1024]{1,0:T(8,128)S(1)}, f32[16,1024]{1,0:T(8,128)S(1)}, u32[]{:S(2)}, u32[]{:S(2)}) collective-permute-start(f32[16,1024]{1,0:T(8,128)S(1)} %multiply_add_fusion.1), channel_id=1, source_target_pairs={{0,256},{8,264},{16,272},{24,280},{32,288},{40,296},{48,304},{56,3... | collective-permute-start | bytes 196616 | tf_op jit(solution)/shard_map/ppermute | solution.py:41
  106.6 11.1 %collective-permute-start.9 = (f32[16,1024]{1,0:T(8,128)S(1)}, f32[16,1024]{1,0:T(8,128)S(1)}, u32[]{:S(2)}, u32[]{:S(2)}) collective-permute-start(f32[16,1024]{1,0:T(8,128)S(1)} %multiply_add_fusion.1), channel_id=1, source_target_pairs={{0,384},{8,392},{16,400},{24,408},{32,416},{40,424},{48,432},{56,4... | collective-permute-start | bytes 196616 | tf_op jit(solution)/shard_map/ppermute | solution.py:41
  112.8 6.5 %copy-start.5 = (f32[1024]{0:T(1024)S(1)}, f32[1024]{0:T(1024)}, u32[]{:S(2)}) copy-start(f32[1024]{0:T(1024)} %param.11) | copy-start | bytes 12292
